TPU v7x, 256 devices: a whole 4x4x8 slice. The times are simulated.
256 devices in a mesh: gx: 8 (over y, core), gy: 8 (over z), ba: 4 (over x).
Axes of the slice: x: 4, y: 4, z: 8, core: 2. Of those that a mesh axis runs over, the one named last changes fastest.
Arguments:
- pixels: float32 [224, 128, 1024], P('ba', 'gy', 'gx'), may hold values from -8 to 8
- spectra: float32 [224, 256], P('ba'), may hold values from -0.375 to 0.375
- abundance: float32 [256, 128, 1024], P('ba', 'gy', 'gx'), may hold values from 0 to 1
- plan: int32 [3], replicated, may hold values from 0 to 1, as said below
Outputs:
- sparse: float32 [256, 128, 1024], P('ba', 'gy', 'gx')
- spectra_grad: float32 [224, 256], P('ba')
Inputs may be any that keep to these rules, and one draw needn't show every extreme that they name: `plan`: entry 0 is 1 and at least one later entry is 0.
All inputs are finite; a program needn't handle non-finite values. Where the computation divides by a largest or mean magnitude, that divisor is 1e-20 or more.
Results may differ from a plain program's by a relative error of at most 0.0001.
Values sent between devices are 32-bit elements; how exact they have to be, the bound alone decides.
No kernel may reach another device: no remote copies, remote signals or barrier semaphores. Data moves between devices by JAX's collectives and lax.ppermute only.
A program may use at most 64 MiB of HBM per device.

v0:
```python
import math

import jax
import jax.numpy as jnp
from jax import lax
from jax.sharding import PartitionSpec as P

SWEEPS = 3


HIGHEST = lax.Precision.HIGHEST
penalty = 1.0
tv_weight = 0.2
sparsity = 0.05

ROWS = ("gy", "ba")


def shifted(x, axes, size, offset):
    pairs = [(i, i + offset) for i in range(size) if 0 <= i + offset < size]
    return lax.ppermute(x, axes, pairs)


def shifted_2(x, axes, sizes, offsets):
    (n0, n1), (d0, d1) = sizes, offsets
    pairs = [
        (i * n1 + j, (i + d0) * n1 + j + d1)
        for i in range(n0)
        for j in range(n1)
        if 0 <= i + d0 < n0 and 0 <= j + d1 < n1
    ]
    return lax.ppermute(x, axes, pairs)


def extended_1(x, col_axis, col_ways, row_axes, row_ways):
    comps, rows, cols = x.shape
    both = (col_axis,) + row_axes
    both_ways = (col_ways, row_ways)
    up = shifted(x[:, rows - 1 :, :], row_axes, row_ways, 1)
    down = shifted(x[:, :1, :], row_axes, row_ways, -1)
    left = shifted(x[:, :, cols - 1 :], col_axis, col_ways, 1)
    right = shifted(x[:, :, :1], col_axis, col_ways, -1)
    top_right = shifted_2(x[:, rows - 1 :, :1], both, both_ways, (-1, 1))
    bottom_left = shifted_2(x[:, :1, cols - 1 :], both, both_ways, (1, -1))
    pad = jnp.zeros((comps, 1, 1), x.dtype)
    top = jnp.concatenate([pad, up, top_right], axis=2)
    middle = jnp.concatenate([left, x, right], axis=2)
    bottom = jnp.concatenate([bottom_left, down, pad], axis=2)
    return jnp.concatenate([top, middle, bottom], axis=1)


def edge_masks(top_row, left_col, row_count, col_count, grid_rows, grid_cols):
    ext_rows = top_row - 1 + jnp.arange(row_count + 1)
    ext_cols = left_col - 1 + jnp.arange(col_count + 1)
    rows_in = (ext_rows >= 0) & (ext_rows <= grid_rows - 1)
    cols_in = (ext_cols >= 0) & (ext_cols <= grid_cols - 1)
    rows_ok = (ext_rows >= 0) & (ext_rows <= grid_rows - 2)
    cols_ok = (ext_cols >= 0) & (ext_cols <= grid_cols - 2)
    mask_h = (rows_in[:, None] & cols_ok[None, :]).astype(jnp.float32)[None]
    mask_v = (rows_ok[:, None] & cols_in[None, :]).astype(jnp.float32)[None]
    return (mask_h, mask_v)


def total_of(x, axes=("ba", "gy", "gx")):
    for axis in axes:
        size = lax.axis_size(axis)
        step = 1
        while step < size:
            x = x + lax.ppermute(x, axis, [(i, i ^ step) for i in range(size)])
            step *= 2
    return x


def total_everywhere(x):
    axes = ("gx", "gy", "ba")
    size = 1
    for axis in axes:
        size *= lax.axis_size(axis)
    return jnp.sum(lax.all_to_all(jnp.broadcast_to(x, (size,)), axes, 0, 0, tiled=True))


def scatter_everywhere(x, axes):
    size = 1
    for axis in axes:
        size *= lax.axis_size(axis)
    parts = x.reshape((size, -1))
    return jnp.sum(lax.all_to_all(parts[:, None], axes, 0, 1, tiled=True)[0], axis=0)


def gathered(x, axes):
    size = 1
    for axis in axes:
        size *= lax.axis_size(axis)
    spread = jnp.broadcast_to(x[None], (size,) + x.shape)
    return lax.all_to_all(spread, axes, 0, 0, tiled=True)


def local(pixels, spectra, abundance, plan):
    band_ways = lax.axis_size("ba")
    row_ways = lax.axis_size("gy") * band_ways
    field = lax.all_to_all(abundance, "ba", 1, 0, tiled=True)
    bands = lax.all_to_all(pixels, "ba", 1, 0, tiled=True)
    all_comps, row_count, gx_cols = field.shape
    grid_rows = row_count * row_ways
    grid_cols = gx_cols * lax.axis_size("gx")
    row_block = lax.axis_index("gy") * band_ways + lax.axis_index("ba")
    top_row = row_block * row_count
    all_spectra = gathered(spectra, ("ba",)).reshape((-1,) + spectra.shape[1:])
    gram = jnp.dot(all_spectra.T, all_spectra, precision=HIGHEST)
    bound = jnp.max(jnp.sum(jnp.abs(gram), axis=1))
    left_col = lax.axis_index("gx") * gx_cols
    mask_h, mask_v = edge_masks(top_row, left_col, row_count, gx_cols, grid_rows, grid_cols)
    sparse = field
    dual = jnp.zeros_like(field)
    weight = jnp.ones((all_comps, row_count + 1, gx_cols + 1), jnp.float32)
    for sweep in range(SWEEPS):
        extended = extended_1(field, "gx", lax.axis_size("gx"), ROWS, row_ways)
        center = extended[:, : row_count + 1, : gx_cols + 1]
        right = extended[:, : row_count + 1, 1:]
        below = extended[:, 1:, : gx_cols + 1]
        diff_h = (right - center) * mask_h
        diff_v = (below - center) * mask_v

        energy = diff_h * diff_h + diff_v * diff_v
        local_total = jnp.sum(energy[:, 1:, 1:])
        if sweep == 0:
            total = total_everywhere(local_total)
        else:
            total = lax.cond(plan[sweep] == 1, total_everywhere, lambda x: x, local_total)
        smooth_sq = total / (all_comps * grid_rows * grid_cols) + 1e-06
        fresh = 1.0 / jnp.sqrt(energy + smooth_sq)
        weight = fresh if sweep == 0 else jnp.where(plan[sweep] == 1, fresh, weight)
        flux_h = weight * diff_h
        flux_v = weight * diff_v
        edge_h = weight * mask_h
        edge_v = weight * mask_v
        tv_grad = flux_h[:, 1:, :-1] - flux_h[:, 1:, 1:] + flux_v[:, :-1, 1:] - flux_v[:, 1:, 1:]
        degree = edge_h[:, 1:, 1:] + edge_h[:, 1:, :-1] + edge_v[:, 1:, 1:] + edge_v[:, :-1, 1:]
        resid = jnp.einsum("lq,qrc->lrc", all_spectra, field, precision=HIGHEST) - bands
        data_grad = jnp.einsum("lp,lrc->prc", all_spectra, resid, precision=HIGHEST)
        grad_total = data_grad + tv_weight * tv_grad + penalty * (field - sparse + dual)
        field = field - grad_total / (bound + penalty + 2.0 * tv_weight * degree)
        sparse = jnp.maximum(field + dual - sparsity / penalty, 0.0)
        dual = dual + field - sparse
    resid = jnp.einsum("lp,prc->lrc", all_spectra, sparse, precision=HIGHEST) - bands
    partial_grad = jnp.einsum("lrc,prc->lp", resid, sparse, precision=HIGHEST) / math.sqrt(
        grid_rows * grid_cols
    )
    block = scatter_everywhere(partial_grad, ("ba", "gx", "gy"))
    spectra_grad = gathered(block, ("gx", "gy")).reshape((-1,) + partial_grad.shape[1:])
    out = lax.all_to_all(sparse, "ba", 0, 1, tiled=True)
    return (out, spectra_grad)


def solution(mesh):
    return jax.shard_map(
        local,
        mesh=mesh,
        in_specs=(P("ba", "gy", "gx"), P("ba", None), P("ba", "gy", "gx"), P()),
        out_specs=(P("ba", "gy", "gx"), P("ba", None)),
        check_vma=False,
    )
```

profile of v0, /device:TPU:2, one launch (start us, length us, event | category | flops | bytes accessed | tf_op | source)
XLA Modules:
  0.0 220.9 jit_solution(9985150953704236830)
XLA Ops:
  0.6 2.0 copy.91
  2.6 5.8 %all-to-all-start.2 = ((f32[64,16,128]{2,0,1:T(8,128)}), f32[64,16,128]{2,0,1:T(8,128)S(1)}, u32[]{:S(2)}, u32[]{:S(2)}) async-start(f32[64,16,128]{2,0,1:T(8,128)} %copy.91), calls=%async_computation.2 | async-start | bytes 1048576 | tf_op jit(solution)/shard_map/all_to_all | solution.py:101
  11.4 4.2 %all-to-all-done.2 = f32[64,16,128]{2,0,1:T(8,128)S(1)} async-done(((f32[64,16,128]{2,0,1:T(8,128)}), f32[64,16,128]{2,0,1:T(8,128)S(1)}, u32[]{:S(2)}, u32[]{:S(2)}) %all-to-all-start.2) | async-done | bytes 524320 | tf_op jit(solution)/shard_map/all_to_all | solution.py:101
  16.3 4.8 %all-to-all-start.3 = ((f32[4,56,256]{2,1,0:T(8,128)}), f32[4,56,256]{2,1,0:T(8,128)S(1)}, u32[]{:S(2)}, u32[]{:S(2)}) async-start(f32[4,56,256]{2,1,0:T(8,128)} %broadcast_in_dim.10), calls=%async_computation.3 | async-start | bytes 458752 | tf_op jit(solution)/shard_map/all_to_all | solution.py:95
  21.4 3.4 %collective-permute-start = (f32[256,1,128]{0,2,1:T(8,128)S(1)}, f32[256,1,128]{0,2,1:T(8,128)S(1)}, u32[]{:S(2)}, u32[]{:S(2)}) collective-permute-start(f32[256,1,128]{0,2,1:T(8,128)S(1)} %get-tuple-element.49), channel_id=1, source_target_pairs={{0,1},{1,2},{2,3},{3,4},{4,5},{5,6},{6,7},{7,8},{8,9},{9,10},{10,1... | collective-permute-start | bytes 393224 | tf_op jit(solution)/shard_map/ppermute | solution.py:21
  24.8 1.4 all-to-all-done.3
  26.2 5.7 %all-to-all-start.4 = ((f32[56,16,128]{2,0,1:T(8,128)}), f32[56,16,128]{2,0,1:T(8,128)S(1)}, u32[]{:S(2)}, u32[]{:S(2)}) async-start(f32[56,16,128]{2,0,1:T(8,128)} %copy.93), calls=%async_computation.4 | async-start | bytes 917504 | tf_op jit(solution)/shard_map/all_to_all | solution.py:102
  35.8 1.9 collective-permute-start.5
  39.7 4.0 %collective-permute-start.4 = (f32[256,1,1]{0,2,1:T(1,128)S(1)}, f32[256,1,1]{0,2,1:T(1,128)S(1)}, u32[]{:S(2)}, u32[]{:S(2)}) collective-permute-start(f32[256,1,1]{0,2,1:T(1,128)S(1)} %get-tuple-element.46), channel_id=1, source_target_pairs={{1,32},{2,33},{3,34},{4,35},{5,36},{6,37},{7,38},{8,39},{9,40},{10... | collective-permute-start | bytes 3080 | tf_op jit(solution)/shard_map/ppermute | solution.py:32
  46.1 1.4 broadcast_in_dim.11
  47.4 22.6 %all-to-all-start.5 = ((f32[256,1,1]{2,1,0:T(1,128)}), f32[256,1,1]{2,1,0:T(1,128)S(1)}, u32[]{:S(2)}, u32[]{:S(2)}) async-start(f32[256,1,1]{2,1,0:T(1,128)} %broadcast_in_dim.11), calls=%async_computation.5 | async-start | bytes 262144 | tf_op jit(solution)/shard_map/all_to_all | solution.py:79
  71.4 10.2 %all-to-all-done.5 = f32[256,1,1]{2,1,0:T(1,128)S(1)} async-done(((f32[256,1,1]{2,1,0:T(1,128)}), f32[256,1,1]{2,1,0:T(1,128)S(1)}, u32[]{:S(2)}, u32[]{:S(2)}) %all-to-all-start.5) | async-done | bytes 1056 | tf_op jit(solution)/shard_map/all_to_all | solution.py:79
  85.5 3.1 %collective-permute-start.6 = (f32[256,1,128]{0,2,1:T(8,128)S(1)}, f32[256,1,128]{0,2,1:T(8,128)S(1)}, u32[]{:S(2)}, u32[]{:S(2)}) collective-permute-start(f32[256,1,128]{0,2,1:T(8,128)S(1)} %get-tuple-element.43), channel_id=1, source_target_pairs={{0,1},{1,2},{2,3},{3,4},{4,5},{5,6},{6,7},{7,8},{8,9},{9,10},{10,1... | collective-permute-start | bytes 393224 | tf_op jit(solution)/shard_map/ppermute | solution.py:21
  88.6 1.6 collective-permute-start.8
  92.8 2.4 %collective-permute-start.11 = (f32[256,1,128]{0,2,1:T(8,128)S(1)}, f32[256,1,128]{0,2,1:T(8,128)S(1)}, u32[]{:S(2)}, u32[]{:S(2)}) collective-permute-start(f32[256,1,128]{0,2,1:T(8,128)S(1)} %get-tuple-element.42), channel_id=1, source_target_pairs={{1,0},{2,1},{3,2},{4,3},{5,4},{6,5},{7,6},{8,7},{9,8},{10,9},{11,1... | collective-permute-start | bytes 393224 | tf_op jit(solution)/shard_map/ppermute | solution.py:21
  95.2 1.5 fusion.15
  96.7 3.2 %collective-permute-start.10 = (f32[256,1,1]{0,2,1:T(1,128)S(1)}, f32[256,1,1]{0,2,1:T(1,128)S(1)}, u32[]{:S(2)}, u32[]{:S(2)}) collective-permute-start(f32[256,1,1]{0,2,1:T(1,128)S(1)} %get-tuple-element.40), channel_id=1, source_target_pairs={{1,32},{2,33},{3,34},{4,35},{5,36},{6,37},{7,38},{8,39},{9,40},{10... | collective-permute-start | bytes 3080 | tf_op jit(solution)/shard_map/ppermute | solution.py:32
  102.5 29.2 %conditional.2 = (f32[]{:T(128)}) conditional(s32[]{:T(128)} %convert_element_type.22, f32[]{:T(128)} %slice_reduce_fusion.1, f32[]{:T(128)} %slice_reduce_fusion.1), branch_computations={%region_5.0_spmd, %region_6.0_spmd} | conditional | flops 255 | bytes 4116 | solution.py:129
  103.2 27.6 %all_to_all.90 = f32[256,1,1]{2,1,0:T(1,128)S(1)} all-to-all(f32[256,1,1]{2,1,0:T(1,128)S(1)} %broadcast_in_dim.0), channel_id=1, replica_groups=mesh['gx'=8,'gy'=8,'ba'=4] {'gx','gy','ba'}, dimensions={0} | all-to-all | bytes 2048 | tf_op jit(solution)/shard_map/cond/branch_1_fun/all_to_all | solution.py:79
  134.3 1.4 fusion.7
  135.7 3.1 %collective-permute-start.12 = (f32[256,1,128]{0,2,1:T(8,128)S(1)}, f32[256,1,128]{0,2,1:T(8,128)S(1)}, u32[]{:S(2)}, u32[]{:S(2)}) collective-permute-start(f32[256,1,128]{0,2,1:T(8,128)S(1)} %get-tuple-element.37), channel_id=1, source_target_pairs={{0,1},{1,2},{2,3},{3,4},{4,5},{5,6},{6,7},{7,8},{8,9},{9,10},{10,1... | collective-permute-start | bytes 393224 | tf_op jit(solution)/shard_map/ppermute | solution.py:21
  138.8 1.6 collective-permute-start.14
  143.1 2.6 %collective-permute-start.17 = (f32[256,1,128]{0,2,1:T(8,128)S(1)}, f32[256,1,128]{0,2,1:T(8,128)S(1)}, u32[]{:S(2)}, u32[]{:S(2)}) collective-permute-start(f32[256,1,128]{0,2,1:T(8,128)S(1)} %get-tuple-element.36), channel_id=1, source_target_pairs={{1,0},{2,1},{3,2},{4,3},{5,4},{6,5},{7,6},{8,7},{9,8},{10,9},{11,1... | collective-permute-start | bytes 393224 | tf_op jit(solution)/shard_map/ppermute | solution.py:21
  145.6 1.5 fusion.16
  147.1 3.2 %collective-permute-start.16 = (f32[256,1,1]{0,2,1:T(1,128)S(1)}, f32[256,1,1]{0,2,1:T(1,128)S(1)}, u32[]{:S(2)}, u32[]{:S(2)}) collective-permute-start(f32[256,1,1]{0,2,1:T(1,128)S(1)} %get-tuple-element.34), channel_id=1, source_target_pairs={{1,32},{2,33},{3,34},{4,35},{5,36},{6,37},{7,38},{8,39},{9,40},{10... | collective-permute-start | bytes 3080 | tf_op jit(solution)/shard_map/ppermute | solution.py:32
  156.5 1.5 fusion.14
  160.5 16.3 %all-to-all-start.7 = ((f32[256,1,224]{2,1,0:T(1,128)}), f32[256,1,224]{2,1,0:T(1,128)S(1)}, u32[]{:S(2)}, u32[]{:S(2)}) async-start(f32[256,1,224]{2,1,0:T(1,128)} %broadcast_in_dim_reshape.4), calls=%async_computation.7 | async-start | bytes 524288 | tf_op jit(solution)/shard_map/all_to_all | solution.py:87
  177.8 13.9 %all-to-all-done.7 = f32[256,1,224]{2,1,0:T(1,128)S(1)} async-done(((f32[256,1,224]{2,1,0:T(1,128)}), f32[256,1,224]{2,1,0:T(1,128)S(1)}, u32[]{:S(2)}, u32[]{:S(2)}) %all-to-all-start.7) | async-done | bytes 229408 | tf_op jit(solution)/shard_map/all_to_all | solution.py:87
  191.7 4.9 %all-to-all-start.6 = ((f32[256,4,128]{2,1,0:T(4,128)}), f32[256,4,128]{2,1,0:T(4,128)S(1)}, u32[]{:S(2)}, u32[]{:S(2)}) async-start(f32[256,4,128]{2,1,0:T(4,128)} %copy.108), calls=%async_computation.6 | async-start | bytes 1048576 | tf_op jit(solution)/shard_map/all_to_all | solution.py:151
  196.9 7.9 %all-to-all-done.6 = f32[256,4,128]{2,1,0:T(4,128)S(1)} async-done(((f32[256,4,128]{2,1,0:T(4,128)}), f32[256,4,128]{2,1,0:T(4,128)S(1)}, u32[]{:S(2)}, u32[]{:S(2)}) %all-to-all-start.6) | async-done | bytes 524320 | tf_op jit(solution)/shard_map/all_to_all | solution.py:151
  205.5 4.6 %all-to-all-start.8 = ((f32[64,1,224]{2,1,0:T(1,128)}), f32[64,1,224]{2,1,0:T(1,128)S(1)}, u32[]{:S(2)}, u32[]{:S(2)}) async-start(f32[64,1,224]{2,1,0:T(1,128)} %broadcast_in_dim.13), calls=%async_computation.8 | async-start | bytes 131072 | tf_op jit(solution)/shard_map/all_to_all | solution.py:95
  211.3 8.8 %all-to-all-done.8 = f32[64,1,224]{2,1,0:T(1,128)S(1)} async-done(((f32[64,1,224]{2,1,0:T(1,128)}), f32[64,1,224]{2,1,0:T(1,128)S(1)}, u32[]{:S(2)}, u32[]{:S(2)}) %all-to-all-start.8) | async-done | bytes 57376 | tf_op jit(solution)/shard_map/all_to_all | solution.py:95
  (101 shorter events, 38.0 us)
Async XLA Ops:
  2.6 5.8 %copy-start.5 = (f32[56,16,128]{2,1,0:T(8,128)S(1)}, f32[56,16,128]{2,1,0:T(8,128)}, u32[]{:S(2)}) copy-start(f32[56,16,128]{2,1,0:T(8,128)} %param.8) | copy-start | bytes 1376260
  2.6 13.0 %all-to-all-start.2 = ((f32[64,16,128]{2,0,1:T(8,128)}), f32[64,16,128]{2,0,1:T(8,128)S(1)}, u32[]{:S(2)}, u32[]{:S(2)}) async-start(f32[64,16,128]{2,0,1:T(8,128)} %copy.91), calls=%async_computation.2 | async-start | bytes 1048576 | tf_op jit(solution)/shard_map/all_to_all | solution.py:101
  8.5 0.9 copy-start.10
  8.5 7.1 %copy-start.9 = (f32[56,256]{1,0:T(8,128)S(1)}, f32[56,256]{1,0:T(8,128)}, u32[]{:S(2)}) copy-start(f32[56,256]{1,0:T(8,128)} %param.9) | copy-start | bytes 172036
  16.3 9.9 %all-to-all-start.3 = ((f32[4,56,256]{2,1,0:T(8,128)}), f32[4,56,256]{2,1,0:T(8,128)S(1)}, u32[]{:S(2)}, u32[]{:S(2)}) async-start(f32[4,56,256]{2,1,0:T(8,128)} %broadcast_in_dim.10), calls=%async_computation.3 | async-start | bytes 458752 | tf_op jit(solution)/shard_map/all_to_all | solution.py:95
  21.4 22.3 %collective-permute-start = (f32[256,1,128]{0,2,1:T(8,128)S(1)}, f32[256,1,128]{0,2,1:T(8,128)S(1)}, u32[]{:S(2)}, u32[]{:S(2)}) collective-permute-start(f32[256,1,128]{0,2,1:T(8,128)S(1)} %get-tuple-element.49), channel_id=1, source_target_pairs={{0,1},{1,2},{2,3},{3,4},{4,5},{5,6},{6,7},{7,8},{8,9},{9,10},{10,1... | collective-permute-start | bytes 393224 | tf_op jit(solution)/shard_map/ppermute | solution.py:21
  26.2 13.5 %all-to-all-start.4 = ((f32[56,16,128]{2,0,1:T(8,128)}), f32[56,16,128]{2,0,1:T(8,128)S(1)}, u32[]{:S(2)}, u32[]{:S(2)}) async-start(f32[56,16,128]{2,0,1:T(8,128)} %copy.93), calls=%async_computation.4 | async-start | bytes 917504 | tf_op jit(solution)/shard_map/all_to_all | solution.py:102
  31.9 11.8 %collective-permute-start.2 = (f32[256,4,1]{0,2,1:T(1,128)S(1)}, f32[256,4,1]{0,2,1:T(1,128)S(1)}, u32[]{:S(2)}, u32[]{:S(2)}) collective-permute-start(f32[256,4,1]{0,2,1:T(1,128)S(1)} %get-tuple-element.50), channel_id=1, source_target_pairs={{0,32},{32,64},{64,96},{96,128},{128,160},{160,192},{192,224},{1,3... | collective-permute-start | bytes 12296 | tf_op jit(solution)/shard_map/ppermute | solution.py:21
  33.2 10.5 %collective-permute-start.3 = (f32[256,4,1]{0,2,1:T(1,128)S(1)}, f32[256,4,1]{0,2,1:T(1,128)S(1)}, u32[]{:S(2)}, u32[]{:S(2)}) collective-permute-start(f32[256,4,1]{0,2,1:T(1,128)S(1)} %get-tuple-element.51), channel_id=1, source_target_pairs={{32,0},{64,32},{96,64},{128,96},{160,128},{192,160},{224,192},{33,... | collective-permute-start | bytes 12296 | tf_op jit(solution)/shard_map/ppermute | solution.py:21
  34.5 5.2 %collective-permute-start.1 = (f32[256,1,1]{0,2,1:T(1,128)S(1)}, f32[256,1,1]{0,2,1:T(1,128)S(1)}, u32[]{:S(2)}, u32[]{:S(2)}) collective-permute-start(f32[256,1,1]{0,2,1:T(1,128)S(1)} %get-tuple-element.47), channel_id=1, source_target_pairs={{32,1},{33,2},{34,3},{35,4},{36,5},{37,6},{38,7},{39,8},{40,9},{41... | collective-permute-start | bytes 3080 | tf_op jit(solution)/shard_map/ppermute | solution.py:32
  35.8 9.2 %collective-permute-start.5 = (f32[256,1,128]{0,2,1:T(8,128)S(1)}, f32[256,1,128]{0,2,1:T(8,128)S(1)}, u32[]{:S(2)}, u32[]{:S(2)}) collective-permute-start(f32[256,1,128]{0,2,1:T(8,128)S(1)} %get-tuple-element.48), channel_id=1, source_target_pairs={{1,0},{2,1},{3,2},{4,3},{5,4},{6,5},{7,6},{8,7},{9,8},{10,9},{11,1... | collective-permute-start | bytes 393224 | tf_op jit(solution)/shard_map/ppermute | solution.py:21
  39.7 5.3 %collective-permute-start.4 = (f32[256,1,1]{0,2,1:T(1,128)S(1)}, f32[256,1,1]{0,2,1:T(1,128)S(1)}, u32[]{:S(2)}, u32[]{:S(2)}) collective-permute-start(f32[256,1,1]{0,2,1:T(1,128)S(1)} %get-tuple-element.46), channel_id=1, source_target_pairs={{1,32},{2,33},{3,34},{4,35},{5,36},{6,37},{7,38},{8,39},{9,40},{10... | collective-permute-start | bytes 3080 | tf_op jit(solution)/shard_map/ppermute | solution.py:32
  47.4 34.1 %all-to-all-start.5 = ((f32[256,1,1]{2,1,0:T(1,128)}), f32[256,1,1]{2,1,0:T(1,128)S(1)}, u32[]{:S(2)}, u32[]{:S(2)}) async-start(f32[256,1,1]{2,1,0:T(1,128)} %broadcast_in_dim.11), calls=%async_computation.5 | async-start | bytes 262144 | tf_op jit(solution)/shard_map/all_to_all | solution.py:79
  83.1 1.0 copy-start.8
  85.5 14.4 %collective-permute-start.6 = (f32[256,1,128]{0,2,1:T(8,128)S(1)}, f32[256,1,128]{0,2,1:T(8,128)S(1)}, u32[]{:S(2)}, u32[]{:S(2)}) collective-permute-start(f32[256,1,128]{0,2,1:T(8,128)S(1)} %get-tuple-element.43), channel_id=1, source_target_pairs={{0,1},{1,2},{2,3},{3,4},{4,5},{5,6},{6,7},{7,8},{8,9},{9,10},{10,1... | collective-permute-start | bytes 393224 | tf_op jit(solution)/shard_map/ppermute | solution.py:21
  88.6 11.2 %collective-permute-start.8 = (f32[256,4,1]{0,2,1:T(1,128)S(1)}, f32[256,4,1]{0,2,1:T(1,128)S(1)}, u32[]{:S(2)}, u32[]{:S(2)}) collective-permute-start(f32[256,4,1]{0,2,1:T(1,128)S(1)} %get-tuple-element.44), channel_id=1, source_target_pairs={{0,32},{32,64},{64,96},{96,128},{128,160},{160,192},{192,224},{1,3... | collective-permute-start | bytes 12296 | tf_op jit(solution)/shard_map/ppermute | solution.py:21
  90.2 9.6 %collective-permute-start.9 = (f32[256,4,1]{0,2,1:T(1,128)S(1)}, f32[256,4,1]{0,2,1:T(1,128)S(1)}, u32[]{:S(2)}, u32[]{:S(2)}) collective-permute-start(f32[256,4,1]{0,2,1:T(1,128)S(1)} %get-tuple-element.45), channel_id=1, source_target_pairs={{32,0},{64,32},{96,64},{128,96},{160,128},{192,160},{224,192},{33,... | collective-permute-start | bytes 12296 | tf_op jit(solution)/shard_map/ppermute | solution.py:21
  91.5 5.2 %collective-permute-start.7 = (f32[256,1,1]{0,2,1:T(1,128)S(1)}, f32[256,1,1]{0,2,1:T(1,128)S(1)}, u32[]{:S(2)}, u32[]{:S(2)}) collective-permute-start(f32[256,1,1]{0,2,1:T(1,128)S(1)} %get-tuple-element.41), channel_id=1, source_target_pairs={{32,1},{33,2},{34,3},{35,4},{36,5},{37,6},{38,7},{39,8},{40,9},{41... | collective-permute-start | bytes 3080 | tf_op jit(solution)/shard_map/ppermute | solution.py:32
  92.8 8.3 %collective-permute-start.11 = (f32[256,1,128]{0,2,1:T(8,128)S(1)}, f32[256,1,128]{0,2,1:T(8,128)S(1)}, u32[]{:S(2)}, u32[]{:S(2)}) collective-permute-start(f32[256,1,128]{0,2,1:T(8,128)S(1)} %get-tuple-element.42), channel_id=1, source_target_pairs={{1,0},{2,1},{3,2},{4,3},{5,4},{6,5},{7,6},{8,7},{9,8},{10,9},{11,1... | collective-permute-start | bytes 393224 | tf_op jit(solution)/shard_map/ppermute | solution.py:21
  96.7 4.4 %collective-permute-start.10 = (f32[256,1,1]{0,2,1:T(1,128)S(1)}, f32[256,1,1]{0,2,1:T(1,128)S(1)}, u32[]{:S(2)}, u32[]{:S(2)}) collective-permute-start(f32[256,1,1]{0,2,1:T(1,128)S(1)} %get-tuple-element.40), channel_id=1, source_target_pairs={{1,32},{2,33},{3,34},{4,35},{5,36},{6,37},{7,38},{8,39},{9,40},{10... | collective-permute-start | bytes 3080 | tf_op jit(solution)/shard_map/ppermute | solution.py:32
  133.3 1.0 copy-start.7
  135.7 14.5 %collective-permute-start.12 = (f32[256,1,128]{0,2,1:T(8,128)S(1)}, f32[256,1,128]{0,2,1:T(8,128)S(1)}, u32[]{:S(2)}, u32[]{:S(2)}) collective-permute-start(f32[256,1,128]{0,2,1:T(8,128)S(1)} %get-tuple-element.37), channel_id=1, source_target_pairs={{0,1},{1,2},{2,3},{3,4},{4,5},{5,6},{6,7},{7,8},{8,9},{9,10},{10,1... | collective-permute-start | bytes 393224 | tf_op jit(solution)/shard_map/ppermute | solution.py:21
  138.8 11.4 %collective-permute-start.14 = (f32[256,4,1]{0,2,1:T(1,128)S(1)}, f32[256,4,1]{0,2,1:T(1,128)S(1)}, u32[]{:S(2)}, u32[]{:S(2)}) collective-permute-start(f32[256,4,1]{0,2,1:T(1,128)S(1)} %get-tuple-element.38), channel_id=1, source_target_pairs={{0,32},{32,64},{64,96},{96,128},{128,160},{160,192},{192,224},{1,3... | collective-permute-start | bytes 12296 | tf_op jit(solution)/shard_map/ppermute | solution.py:21
  140.5 9.8 %collective-permute-start.15 = (f32[256,4,1]{0,2,1:T(1,128)S(1)}, f32[256,4,1]{0,2,1:T(1,128)S(1)}, u32[]{:S(2)}, u32[]{:S(2)}) collective-permute-start(f32[256,4,1]{0,2,1:T(1,128)S(1)} %get-tuple-element.39), channel_id=1, source_target_pairs={{32,0},{64,32},{96,64},{128,96},{160,128},{192,160},{224,192},{33,... | collective-permute-start | bytes 12296 | tf_op jit(solution)/shard_map/ppermute | solution.py:21
  141.8 5.3 %collective-permute-start.13 = (f32[256,1,1]{0,2,1:T(1,128)S(1)}, f32[256,1,1]{0,2,1:T(1,128)S(1)}, u32[]{:S(2)}, u32[]{:S(2)}) collective-permute-start(f32[256,1,1]{0,2,1:T(1,128)S(1)} %get-tuple-element.35), channel_id=1, source_target_pairs={{32,1},{33,2},{34,3},{35,4},{36,5},{37,6},{38,7},{39,8},{40,9},{41... | collective-permute-start | bytes 3080 | tf_op jit(solution)/shard_map/ppermute | solution.py:32
  143.1 8.5 %collective-permute-start.17 = (f32[256,1,128]{0,2,1:T(8,128)S(1)}, f32[256,1,128]{0,2,1:T(8,128)S(1)}, u32[]{:S(2)}, u32[]{:S(2)}) collective-permute-start(f32[256,1,128]{0,2,1:T(8,128)S(1)} %get-tuple-element.36), channel_id=1, source_target_pairs={{1,0},{2,1},{3,2},{4,3},{5,4},{6,5},{7,6},{8,7},{9,8},{10,9},{11,1... | collective-permute-start | bytes 393224 | tf_op jit(solution)/shard_map/ppermute | solution.py:21
  147.1 4.4 %collective-permute-start.16 = (f32[256,1,1]{0,2,1:T(1,128)S(1)}, f32[256,1,1]{0,2,1:T(1,128)S(1)}, u32[]{:S(2)}, u32[]{:S(2)}) collective-permute-start(f32[256,1,1]{0,2,1:T(1,128)S(1)} %get-tuple-element.34), channel_id=1, source_target_pairs={{1,32},{2,33},{3,34},{4,35},{5,36},{6,37},{7,38},{8,39},{9,40},{10... | collective-permute-start | bytes 3080 | tf_op jit(solution)/shard_map/ppermute | solution.py:32
  152.7 1.4 copy-start.1
  155.5 1.0 copy-start.6
  160.5 31.2 %all-to-all-start.7 = ((f32[256,1,224]{2,1,0:T(1,128)}), f32[256,1,224]{2,1,0:T(1,128)S(1)}, u32[]{:S(2)}, u32[]{:S(2)}) async-start(f32[256,1,224]{2,1,0:T(1,128)} %broadcast_in_dim_reshape.4), calls=%async_computation.7 | async-start | bytes 524288 | tf_op jit(solution)/shard_map/all_to_all | solution.py:87
  191.7 13.1 %all-to-all-start.6 = ((f32[256,4,128]{2,1,0:T(4,128)}), f32[256,4,128]{2,1,0:T(4,128)S(1)}, u32[]{:S(2)}, u32[]{:S(2)}) async-start(f32[256,4,128]{2,1,0:T(4,128)} %copy.108), calls=%async_computation.6 | async-start | bytes 1048576 | tf_op jit(solution)/shard_map/all_to_all | solution.py:151
  205.5 14.5 %all-to-all-start.8 = ((f32[64,1,224]{2,1,0:T(1,128)}), f32[64,1,224]{2,1,0:T(1,128)S(1)}, u32[]{:S(2)}, u32[]{:S(2)}) async-start(f32[64,1,224]{2,1,0:T(1,128)} %broadcast_in_dim.13), calls=%async_computation.8 | async-start | bytes 131072 | tf_op jit(solution)/shard_map/all_to_all | solution.py:95
  (4 other events, 3.3 us)
where the time goes:
time: 223 us; the launch traced here: 221 us
  starting transfers between devices  104 us (47%)
  waiting for transfers between devices  49.9 us (22%)
  blocking collectives  27.6 us (12%)
  local copies, waits for them, and re-layouts  15.3 us (7%)
  matrix products  10.5 us (5%)
  other arithmetic  8.88 us (4%)
  between operations  5 us (2%)
    all_to_all x1, blocking collectives, total_everywhere(): lax.all_to_all(jnp.broadcast_to(x, (size,)), axes, 0, 0, tiled=True)  27.6 us
    ppermute x12, starting transfers between devices, shifted(): return lax.ppermute(x, axes, pairs)  24.8 us
    all_to_all x1, starting transfers between devices, total_everywhere(): lax.all_to_all(jnp.broadcast_to(x, (size,)), axes, 0, 0, tiled=True)  22.6 us
    all_to_all x1, starting transfers between devices, scatter_everywhere(): lax.all_to_all(parts[:, None], axes, 0, 1, tiled=True)[0]  16.3 us
    ppermute x6, starting transfers between devices, shifted_2(): return lax.ppermute(x, axes, pairs)  14.2 us
    all_to_all x1, waiting for transfers between devices, scatter_everywhere(): lax.all_to_all(parts[:, None], axes, 0, 1, tiled=True)[0]  13.9 us
    all_to_all x1, waiting for transfers between devices, total_everywhere(): lax.all_to_all(jnp.broadcast_to(x, (size,)), axes, 0, 0, tiled=True)  10.2 us
    all_to_all x2, waiting for transfers between devices, gathered(): return lax.all_to_all(spread, axes, 0, 0, tiled=True)  10.1 us
  transfers between devices with their start and end apart: 25, of which 9 were waited for; matrix products, arithmetic and copies ran while one was open for 5% of the time, Pallas kernels for 0%

commit v1 on v0

--- a/solution.py
+++ b/solution.py
@@ -98,14 +98,24 @@
 def local(pixels, spectra, abundance, plan):
     band_ways = lax.axis_size("ba")
     row_ways = lax.axis_size("gy") * band_ways
-    field = lax.all_to_all(abundance, "ba", 1, 0, tiled=True)
-    bands = lax.all_to_all(pixels, "ba", 1, 0, tiled=True)
+    comps, bands_here = abundance.shape[0], pixels.shape[0]
+    rows_here, cols_here = abundance.shape[1:]
+    quarter = rows_here // band_ways
+    lines = spectra.shape[1] // cols_here
+    copy = jnp.zeros((bands_here, quarter, cols_here), spectra.dtype)
+    copy = copy.at[:, :lines].set(spectra.reshape(bands_here, lines, cols_here))
+    sent = jnp.concatenate([abundance, pixels, jnp.tile(copy, (1, band_ways, 1))], axis=0)
+    got = lax.all_to_all(sent, "ba", 1, 0, tiled=True).reshape(
+        (band_ways, comps + 2 * bands_here, quarter, cols_here)
+    )
+    field = got[:, :comps].reshape((band_ways * comps, quarter, cols_here))
+    bands = got[:, comps : comps + bands_here].reshape((band_ways * bands_here, quarter, cols_here))
+    all_spectra = got[:, comps + bands_here :, :lines].reshape((band_ways * bands_here, -1))
     all_comps, row_count, gx_cols = field.shape
     grid_rows = row_count * row_ways
     grid_cols = gx_cols * lax.axis_size("gx")
     row_block = lax.axis_index("gy") * band_ways + lax.axis_index("ba")
     top_row = row_block * row_count
-    all_spectra = gathered(spectra, ("ba",)).reshape((-1,) + spectra.shape[1:])
     gram = jnp.dot(all_spectra.T, all_spectra, precision=HIGHEST)
     bound = jnp.max(jnp.sum(jnp.abs(gram), axis=1))
     left_col = lax.axis_index("gx") * gx_cols

time: 223 us -> 233 us (1.045)
  waiting for transfers between devices: 49.9 us -> 57.9 us
    all_to_all x2 -> x1, waiting for transfers between devices: 4.25 us -> 14.2 us  [local(): lax.all_to_all(sent, 'ba', 1, 0, tiled=True)]
    ppermute x12, starting transfers between devices: 24.8 us -> 31.5 us  [shifted(): return lax.ppermute(x, axes, pairs)]
    all_to_all x2 -> x1, starting transfers between devices: 11.5 us -> 5.89 us  [local(): lax.all_to_all(sent, 'ba', 1, 0, tiled=True)]
    all_to_all x2 -> x1, starting transfers between devices: 9.39 us -> 4.57 us  [gathered(): return lax.all_to_all(spread, axes, 0, 0, tiled=True)]
    all_to_all x2 -> x1, waiting for transfers between devices: 10.1 us -> 8.75 us  [gathered(): return lax.all_to_all(spread, axes, 0, 0, tiled=True)]
    unnamed x25 -> x34, local copies, waits for them, and re-layouts: 7.89 us -> 7.87 us
  transfers between devices with their start and end apart: 25 -> 23, of which waited for: 9 -> 9; matrix products, arithmetic and copies ran while one was open for 5% -> 4% of each run, Pallas kernels for 0% -> 0%
where the time goes in v1:
time: 233 us; the launch traced here: 231 us
  starting transfers between devices  103 us (44%)
  waiting for transfers between devices  57.9 us (25%)
  blocking collectives  28.3 us (12%)
  local copies, waits for them, and re-layouts  15 us (6%)
  other arithmetic  10.8 us (5%)
  matrix products  10.4 us (4%)
  between operations  5.1 us (2%)
    ppermute x12, starting transfers between devices, shifted(): return lax.ppermute(x, axes, pairs)  31.5 us
    all_to_all x1, blocking collectives, total_everywhere(): lax.all_to_all(jnp.broadcast_to(x, (size,)), axes, 0, 0, tiled=True)  28.3 us
    all_to_all x1, starting transfers between devices, total_everywhere(): lax.all_to_all(jnp.broadcast_to(x, (size,)), axes, 0, 0, tiled=True)  23.7 us
    all_to_all x1, starting transfers between devices, scatter_everywhere(): lax.all_to_all(parts[:, None], axes, 0, 1, tiled=True)[0]  17 us
    ppermute x6, starting transfers between devices, shifted_2(): return lax.ppermute(x, axes, pairs)  15.6 us
    all_to_all x1, waiting for transfers between devices, local(): lax.all_to_all(sent, 'ba', 1, 0, tiled=True)  14.2 us
    all_to_all x1, waiting for transfers between devices, scatter_everywhere(): lax.all_to_all(parts[:, None], axes, 0, 1, tiled=True)[0]  13.9 us
    all_to_all x1, waiting for transfers between devices, total_everywhere(): lax.all_to_all(jnp.broadcast_to(x, (size,)), axes, 0, 0, tiled=True)  9.54 us
  transfers between devices with their start and end apart: 23, of which 9 were waited for; matrix products, arithmetic and copies ran while one was open for 4% of the time, Pallas kernels for 0%

profile of v1, /device:TPU:2, one launch (start us, length us, event | category | flops | bytes accessed | tf_op | source)
XLA Modules:
  0.0 230.6 jit_solution(7046607786567754275)
XLA Ops:
  5.1 5.9 %all-to-all-start.2 = ((f32[176,16,128]{2,0,1:T(8,128)}), f32[176,16,128]{2,0,1:T(8,128)S(1)}, u32[]{:S(2)}, u32[]{:S(2)}) async-start(f32[176,16,128]{2,0,1:T(8,128)} %pad_maximum_fusion), calls=%async_computation.2 | async-start | bytes 2883584 | tf_op jit(solution)/shard_map/all_to_all | solution.py:108
  13.7 14.2 %all-to-all-done.2 = f32[176,16,128]{2,0,1:T(8,128)S(1)} async-done(((f32[176,16,128]{2,0,1:T(8,128)}), f32[176,16,128]{2,0,1:T(8,128)S(1)}, u32[]{:S(2)}, u32[]{:S(2)}) %all-to-all-start.2) | async-done | bytes 1441824 | tf_op jit(solution)/shard_map/all_to_all | solution.py:108
  30.0 2.6 %collective-permute-start.2 = (f32[256,4,1]{0,2,1:T(1,128)S(1)}, f32[256,4,1]{0,2,1:T(1,128)S(1)}, u32[]{:S(2)}, u32[]{:S(2)}) collective-permute-start(f32[256,4,1]{0,2,1:T(1,128)S(1)} %get-tuple-element.62), channel_id=1, source_target_pairs={{0,32},{32,64},{64,96},{96,128},{128,160},{160,192},{192,224},{1,3... | collective-permute-start | bytes 12296 | tf_op jit(solution)/shard_map/ppermute | solution.py:21
  33.9 4.0 %collective-permute-start.5 = (f32[256,1,128]{0,2,1:T(8,128)S(1)}, f32[256,1,128]{0,2,1:T(8,128)S(1)}, u32[]{:S(2)}, u32[]{:S(2)}) collective-permute-start(f32[256,1,128]{0,2,1:T(8,128)S(1)} %get-tuple-element.60), channel_id=1, source_target_pairs={{1,0},{2,1},{3,2},{4,3},{5,4},{6,5},{7,6},{8,7},{9,8},{10,9},{11,1... | collective-permute-start | bytes 393224 | tf_op jit(solution)/shard_map/ppermute | solution.py:21
  37.9 1.9 collective-permute-start
  39.8 1.3 convolution_subtract_fusion.3
  41.2 4.1 %collective-permute-start.4 = (f32[256,1,1]{0,2,1:T(1,128)S(1)}, f32[256,1,1]{0,2,1:T(1,128)S(1)}, u32[]{:S(2)}, u32[]{:S(2)}) collective-permute-start(f32[256,1,1]{0,2,1:T(1,128)S(1)} %get-tuple-element.58), channel_id=1, source_target_pairs={{1,32},{2,33},{3,34},{4,35},{5,36},{6,37},{7,38},{8,39},{9,40},{10... | collective-permute-start | bytes 3080 | tf_op jit(solution)/shard_map/ppermute | solution.py:32
  47.6 1.4 broadcast_in_dim.8
  49.0 23.7 %all-to-all-start.3 = ((f32[256,1,1]{2,1,0:T(1,128)}), f32[256,1,1]{2,1,0:T(1,128)S(1)}, u32[]{:S(2)}, u32[]{:S(2)}) async-start(f32[256,1,1]{2,1,0:T(1,128)} %broadcast_in_dim.8), calls=%async_computation.3 | async-start | bytes 262144 | tf_op jit(solution)/shard_map/all_to_all | solution.py:79
  74.6 9.5 %all-to-all-done.3 = f32[256,1,1]{2,1,0:T(1,128)S(1)} async-done(((f32[256,1,1]{2,1,0:T(1,128)}), f32[256,1,1]{2,1,0:T(1,128)S(1)}, u32[]{:S(2)}, u32[]{:S(2)}) %all-to-all-start.3) | async-done | bytes 1056 | tf_op jit(solution)/shard_map/all_to_all | solution.py:79
  86.7 1.4 fusion.11
  89.4 3.8 %collective-permute-start.8 = (f32[256,4,1]{0,2,1:T(1,128)S(1)}, f32[256,4,1]{0,2,1:T(1,128)S(1)}, u32[]{:S(2)}, u32[]{:S(2)}) collective-permute-start(f32[256,4,1]{0,2,1:T(1,128)S(1)} %get-tuple-element.56), channel_id=1, source_target_pairs={{0,32},{32,64},{64,96},{96,128},{128,160},{160,192},{192,224},{1,3... | collective-permute-start | bytes 12296 | tf_op jit(solution)/shard_map/ppermute | solution.py:21
  94.5 2.8 %collective-permute-start.11 = (f32[256,1,128]{0,2,1:T(8,128)S(1)}, f32[256,1,128]{0,2,1:T(8,128)S(1)}, u32[]{:S(2)}, u32[]{:S(2)}) collective-permute-start(f32[256,1,128]{0,2,1:T(8,128)S(1)} %get-tuple-element.54), channel_id=1, source_target_pairs={{1,0},{2,1},{3,2},{4,3},{5,4},{6,5},{7,6},{8,7},{9,8},{10,9},{11,1... | collective-permute-start | bytes 393224 | tf_op jit(solution)/shard_map/ppermute | solution.py:21
  97.3 3.1 %collective-permute-start.6 = (f32[256,1,128]{0,2,1:T(8,128)S(1)}, f32[256,1,128]{0,2,1:T(8,128)S(1)}, u32[]{:S(2)}, u32[]{:S(2)}) collective-permute-start(f32[256,1,128]{0,2,1:T(8,128)S(1)} %get-tuple-element.55), channel_id=1, source_target_pairs={{0,1},{1,2},{2,3},{3,4},{4,5},{5,6},{6,7},{7,8},{8,9},{9,10},{10,1... | collective-permute-start | bytes 393224 | tf_op jit(solution)/shard_map/ppermute | solution.py:21
  100.4 1.4 convolution_subtract_fusion.2
  101.8 3.7 %collective-permute-start.10 = (f32[256,1,1]{0,2,1:T(1,128)S(1)}, f32[256,1,1]{0,2,1:T(1,128)S(1)}, u32[]{:S(2)}, u32[]{:S(2)}) collective-permute-start(f32[256,1,1]{0,2,1:T(1,128)S(1)} %get-tuple-element.52), channel_id=1, source_target_pairs={{1,32},{2,33},{3,34},{4,35},{5,36},{6,37},{7,38},{8,39},{9,40},{10... | collective-permute-start | bytes 3080 | tf_op jit(solution)/shard_map/ppermute | solution.py:32
  107.9 29.9 %conditional.2 = (f32[]{:T(128)}) conditional(s32[]{:T(128)} %convert_element_type.22, f32[]{:T(128)} %slice_reduce_fusion.1, f32[]{:T(128)} %slice_reduce_fusion.1), branch_computations={%region_5.0_spmd, %region_6.8_spmd} | conditional | flops 255 | bytes 4116 | solution.py:139
  108.6 28.3 %all_to_all.64 = f32[256,1,1]{2,1,0:T(1,128)S(1)} all-to-all(f32[256,1,1]{2,1,0:T(1,128)S(1)} %broadcast_in_dim.0), channel_id=1, replica_groups=mesh['gx'=8,'gy'=8,'ba'=4] {'gx','gy','ba'}, dimensions={0} | all-to-all | bytes 2048 | tf_op jit(solution)/shard_map/cond/branch_1_fun/all_to_all | solution.py:79
  140.4 1.4 fusion.8
  141.8 1.5 collective-permute-start.13
  143.3 3.6 %collective-permute-start.14 = (f32[256,4,1]{0,2,1:T(1,128)S(1)}, f32[256,4,1]{0,2,1:T(1,128)S(1)}, u32[]{:S(2)}, u32[]{:S(2)}) collective-permute-start(f32[256,4,1]{0,2,1:T(1,128)S(1)} %get-tuple-element.50), channel_id=1, source_target_pairs={{0,32},{32,64},{64,96},{96,128},{128,160},{160,192},{192,224},{1,3... | collective-permute-start | bytes 12296 | tf_op jit(solution)/shard_map/ppermute | solution.py:21
  148.3 2.8 %collective-permute-start.17 = (f32[256,1,128]{0,2,1:T(8,128)S(1)}, f32[256,1,128]{0,2,1:T(8,128)S(1)}, u32[]{:S(2)}, u32[]{:S(2)}) collective-permute-start(f32[256,1,128]{0,2,1:T(8,128)S(1)} %get-tuple-element.48), channel_id=1, source_target_pairs={{1,0},{2,1},{3,2},{4,3},{5,4},{6,5},{7,6},{8,7},{9,8},{10,9},{11,1... | collective-permute-start | bytes 393224 | tf_op jit(solution)/shard_map/ppermute | solution.py:21
  151.0 3.1 %collective-permute-start.12 = (f32[256,1,128]{0,2,1:T(8,128)S(1)}, f32[256,1,128]{0,2,1:T(8,128)S(1)}, u32[]{:S(2)}, u32[]{:S(2)}) collective-permute-start(f32[256,1,128]{0,2,1:T(8,128)S(1)} %get-tuple-element.49), channel_id=1, source_target_pairs={{0,1},{1,2},{2,3},{3,4},{4,5},{5,6},{6,7},{7,8},{8,9},{9,10},{10,1... | collective-permute-start | bytes 393224 | tf_op jit(solution)/shard_map/ppermute | solution.py:21
  154.1 1.4 convolution_subtract_fusion.1
  155.6 3.7 %collective-permute-start.16 = (f32[256,1,1]{0,2,1:T(1,128)S(1)}, f32[256,1,1]{0,2,1:T(1,128)S(1)}, u32[]{:S(2)}, u32[]{:S(2)}) collective-permute-start(f32[256,1,1]{0,2,1:T(1,128)S(1)} %get-tuple-element.46), channel_id=1, source_target_pairs={{1,32},{2,33},{3,34},{4,35},{5,36},{6,37},{7,38},{8,39},{9,40},{10... | collective-permute-start | bytes 3080 | tf_op jit(solution)/shard_map/ppermute | solution.py:32
  165.5 1.5 fusion.5
  169.5 17.0 %all-to-all-start.5 = ((f32[256,1,224]{2,1,0:T(1,128)}), f32[256,1,224]{2,1,0:T(1,128)S(1)}, u32[]{:S(2)}, u32[]{:S(2)}) async-start(f32[256,1,224]{2,1,0:T(1,128)} %broadcast_in_dim_reshape.4), calls=%async_computation.5 | async-start | bytes 524288 | tf_op jit(solution)/shard_map/all_to_all | solution.py:87
  187.5 13.9 %all-to-all-done.5 = f32[256,1,224]{2,1,0:T(1,128)S(1)} async-done(((f32[256,1,224]{2,1,0:T(1,128)}), f32[256,1,224]{2,1,0:T(1,128)S(1)}, u32[]{:S(2)}, u32[]{:S(2)}) %all-to-all-start.5) | async-done | bytes 229408 | tf_op jit(solution)/shard_map/all_to_all | solution.py:87
  201.4 4.9 %all-to-all-start.4 = ((f32[256,4,128]{2,1,0:T(4,128)}), f32[256,4,128]{2,1,0:T(4,128)S(1)}, u32[]{:S(2)}, u32[]{:S(2)}) async-start(f32[256,4,128]{2,1,0:T(4,128)} %copy.124), calls=%async_computation.4 | async-start | bytes 1048576 | tf_op jit(solution)/shard_map/all_to_all | solution.py:161
  206.6 7.9 %all-to-all-done.4 = f32[256,4,128]{2,1,0:T(4,128)S(1)} async-done(((f32[256,4,128]{2,1,0:T(4,128)}), f32[256,4,128]{2,1,0:T(4,128)S(1)}, u32[]{:S(2)}, u32[]{:S(2)}) %all-to-all-start.4) | async-done | bytes 524320 | tf_op jit(solution)/shard_map/all_to_all | solution.py:161
  215.2 4.6 %all-to-all-start.6 = ((f32[64,1,224]{2,1,0:T(1,128)}), f32[64,1,224]{2,1,0:T(1,128)S(1)}, u32[]{:S(2)}, u32[]{:S(2)}) async-start(f32[64,1,224]{2,1,0:T(1,128)} %broadcast_in_dim.10), calls=%async_computation.6 | async-start | bytes 131072 | tf_op jit(solution)/shard_map/all_to_all | solution.py:95
  221.0 8.8 %all-to-all-done.6 = f32[64,1,224]{2,1,0:T(1,128)S(1)} async-done(((f32[64,1,224]{2,1,0:T(1,128)}), f32[64,1,224]{2,1,0:T(1,128)S(1)}, u32[]{:S(2)}, u32[]{:S(2)}) %all-to-all-start.6) | async-done | bytes 57376 | tf_op jit(solution)/shard_map/all_to_all | solution.py:95
  (113 shorter events, 36.3 us)
Async XLA Ops:
  5.1 5.9 %copy-start.14 = (s32[3]{0:T(128)S(1)}, s32[3]{0:T(128)}, u32[]{:S(2)}) copy-start(s32[3]{0:T(128)} %param.13) | copy-start | bytes 40
  5.1 22.8 %all-to-all-start.2 = ((f32[176,16,128]{2,0,1:T(8,128)}), f32[176,16,128]{2,0,1:T(8,128)S(1)}, u32[]{:S(2)}, u32[]{:S(2)}) async-start(f32[176,16,128]{2,0,1:T(8,128)} %pad_maximum_fusion), calls=%async_computation.2 | async-start | bytes 2883584 | tf_op jit(solution)/shard_map/all_to_all | solution.py:108
  28.7 12.5 %collective-permute-start.1 = (f32[256,1,1]{0,2,1:T(1,128)S(1)}, f32[256,1,1]{0,2,1:T(1,128)S(1)}, u32[]{:S(2)}, u32[]{:S(2)}) collective-permute-start(f32[256,1,1]{0,2,1:T(1,128)S(1)} %get-tuple-element.59), channel_id=1, source_target_pairs={{32,1},{33,2},{34,3},{35,4},{36,5},{37,6},{38,7},{39,8},{40,9},{41... | collective-permute-start | bytes 3080 | tf_op jit(solution)/shard_map/ppermute | solution.py:32
  30.0 15.3 %collective-permute-start.2 = (f32[256,4,1]{0,2,1:T(1,128)S(1)}, f32[256,4,1]{0,2,1:T(1,128)S(1)}, u32[]{:S(2)}, u32[]{:S(2)}) collective-permute-start(f32[256,4,1]{0,2,1:T(1,128)S(1)} %get-tuple-element.62), channel_id=1, source_target_pairs={{0,32},{32,64},{64,96},{96,128},{128,160},{160,192},{192,224},{1,3... | collective-permute-start | bytes 12296 | tf_op jit(solution)/shard_map/ppermute | solution.py:21
  32.6 12.7 %collective-permute-start.3 = (f32[256,4,1]{0,2,1:T(1,128)S(1)}, f32[256,4,1]{0,2,1:T(1,128)S(1)}, u32[]{:S(2)}, u32[]{:S(2)}) collective-permute-start(f32[256,4,1]{0,2,1:T(1,128)S(1)} %get-tuple-element.63), channel_id=1, source_target_pairs={{32,0},{64,32},{96,64},{128,96},{160,128},{192,160},{224,192},{33,... | collective-permute-start | bytes 12296 | tf_op jit(solution)/shard_map/ppermute | solution.py:21
  33.9 12.6 %collective-permute-start.5 = (f32[256,1,128]{0,2,1:T(8,128)S(1)}, f32[256,1,128]{0,2,1:T(8,128)S(1)}, u32[]{:S(2)}, u32[]{:S(2)}) collective-permute-start(f32[256,1,128]{0,2,1:T(8,128)S(1)} %get-tuple-element.60), channel_id=1, source_target_pairs={{1,0},{2,1},{3,2},{4,3},{5,4},{6,5},{7,6},{8,7},{9,8},{10,9},{11,1... | collective-permute-start | bytes 393224 | tf_op jit(solution)/shard_map/ppermute | solution.py:21
  37.9 8.1 %collective-permute-start = (f32[256,1,128]{0,2,1:T(8,128)S(1)}, f32[256,1,128]{0,2,1:T(8,128)S(1)}, u32[]{:S(2)}, u32[]{:S(2)}) collective-permute-start(f32[256,1,128]{0,2,1:T(8,128)S(1)} %get-tuple-element.61), channel_id=1, source_target_pairs={{0,1},{1,2},{2,3},{3,4},{4,5},{5,6},{6,7},{7,8},{8,9},{9,10},{10,1... | collective-permute-start | bytes 393224 | tf_op jit(solution)/shard_map/ppermute | solution.py:21
  39.8 6.7 %copy-start.9 = (f32[5,129]{1,0:T(8,128)S(1)}, f32[5,129]{1,0:T(8,128)}, u32[]{:S(2)}) copy-start(f32[5,129]{1,0:T(8,128)} %and_convert_fusion) | copy-start | bytes 7744
  41.2 5.4 %collective-permute-start.4 = (f32[256,1,1]{0,2,1:T(1,128)S(1)}, f32[256,1,1]{0,2,1:T(1,128)S(1)}, u32[]{:S(2)}, u32[]{:S(2)}) collective-permute-start(f32[256,1,1]{0,2,1:T(1,128)S(1)} %get-tuple-element.58), channel_id=1, source_target_pairs={{1,32},{2,33},{3,34},{4,35},{5,36},{6,37},{7,38},{8,39},{9,40},{10... | collective-permute-start | bytes 3080 | tf_op jit(solution)/shard_map/ppermute | solution.py:32
  46.0 39.6 %copy-start.12 = (f32[256,1,1]{0,2,1:T(1,128)}, f32[256,1,1]{0,2,1:T(1,128)S(1)}, u32[]{:S(2)}) copy-start(f32[256,1,1]{0,2,1:T(1,128)S(1)} %broadcast.156) | copy-start | bytes 3076
  46.1 39.5 %copy-start.10 = (f32[5,129]{1,0:T(8,128)S(1)}, f32[5,129]{1,0:T(8,128)}, u32[]{:S(2)}) copy-start(f32[5,129]{1,0:T(8,128)} %and_convert_fusion) | copy-start | bytes 7744
  49.0 35.2 %all-to-all-start.3 = ((f32[256,1,1]{2,1,0:T(1,128)}), f32[256,1,1]{2,1,0:T(1,128)S(1)}, u32[]{:S(2)}, u32[]{:S(2)}) async-start(f32[256,1,1]{2,1,0:T(1,128)} %broadcast_in_dim.8), calls=%async_computation.3 | async-start | bytes 262144 | tf_op jit(solution)/shard_map/all_to_all | solution.py:79
  85.6 1.0 copy-start.7
  88.0 17.6 %copy-start.13 = (f32[256,1,1]{0,2,1:T(1,128)S(1)}, f32[256,1,1]{0,2,1:T(1,128)}, u32[]{:S(2)}) copy-start(f32[256,1,1]{0,2,1:T(1,128)} %copy-done.12) | copy-start | bytes 3076
  88.1 13.7 %collective-permute-start.7 = (f32[256,1,1]{0,2,1:T(1,128)S(1)}, f32[256,1,1]{0,2,1:T(1,128)S(1)}, u32[]{:S(2)}, u32[]{:S(2)}) collective-permute-start(f32[256,1,1]{0,2,1:T(1,128)S(1)} %get-tuple-element.53), channel_id=1, source_target_pairs={{32,1},{33,2},{34,3},{35,4},{36,5},{37,6},{38,7},{39,8},{40,9},{41... | collective-permute-start | bytes 3080 | tf_op jit(solution)/shard_map/ppermute | solution.py:32
  89.4 16.2 %collective-permute-start.8 = (f32[256,4,1]{0,2,1:T(1,128)S(1)}, f32[256,4,1]{0,2,1:T(1,128)S(1)}, u32[]{:S(2)}, u32[]{:S(2)}) collective-permute-start(f32[256,4,1]{0,2,1:T(1,128)S(1)} %get-tuple-element.56), channel_id=1, source_target_pairs={{0,32},{32,64},{64,96},{96,128},{128,160},{160,192},{192,224},{1,3... | collective-permute-start | bytes 12296 | tf_op jit(solution)/shard_map/ppermute | solution.py:21
  93.2 12.4 %collective-permute-start.9 = (f32[256,4,1]{0,2,1:T(1,128)S(1)}, f32[256,4,1]{0,2,1:T(1,128)S(1)}, u32[]{:S(2)}, u32[]{:S(2)}) collective-permute-start(f32[256,4,1]{0,2,1:T(1,128)S(1)} %get-tuple-element.57), channel_id=1, source_target_pairs={{32,0},{64,32},{96,64},{128,96},{160,128},{192,160},{224,192},{33,... | collective-permute-start | bytes 12296 | tf_op jit(solution)/shard_map/ppermute | solution.py:21
  94.5 12.3 %collective-permute-start.11 = (f32[256,1,128]{0,2,1:T(8,128)S(1)}, f32[256,1,128]{0,2,1:T(8,128)S(1)}, u32[]{:S(2)}, u32[]{:S(2)}) collective-permute-start(f32[256,1,128]{0,2,1:T(8,128)S(1)} %get-tuple-element.54), channel_id=1, source_target_pairs={{1,0},{2,1},{3,2},{4,3},{5,4},{6,5},{7,6},{8,7},{9,8},{10,9},{11,1... | collective-permute-start | bytes 393224 | tf_op jit(solution)/shard_map/ppermute | solution.py:21
  97.3 9.6 %copy-start.11 = (f32[5,129]{1,0:T(8,128)S(1)}, f32[5,129]{1,0:T(8,128)}, u32[]{:S(2)}) copy-start(f32[5,129]{1,0:T(8,128)} %and_convert_fusion) | copy-start | bytes 7744
  97.3 8.3 %collective-permute-start.6 = (f32[256,1,128]{0,2,1:T(8,128)S(1)}, f32[256,1,128]{0,2,1:T(8,128)S(1)}, u32[]{:S(2)}, u32[]{:S(2)}) collective-permute-start(f32[256,1,128]{0,2,1:T(8,128)S(1)} %get-tuple-element.55), channel_id=1, source_target_pairs={{0,1},{1,2},{2,3},{3,4},{4,5},{5,6},{6,7},{7,8},{8,9},{9,10},{10,1... | collective-permute-start | bytes 393224 | tf_op jit(solution)/shard_map/ppermute | solution.py:21
  101.8 5.0 %collective-permute-start.10 = (f32[256,1,1]{0,2,1:T(1,128)S(1)}, f32[256,1,1]{0,2,1:T(1,128)S(1)}, u32[]{:S(2)}, u32[]{:S(2)}) collective-permute-start(f32[256,1,1]{0,2,1:T(1,128)S(1)} %get-tuple-element.52), channel_id=1, source_target_pairs={{1,32},{2,33},{3,34},{4,35},{5,36},{6,37},{7,38},{8,39},{9,40},{10... | collective-permute-start | bytes 3080 | tf_op jit(solution)/shard_map/ppermute | solution.py:32
  106.8 1.1 copy-start.4
  141.8 13.7 %collective-permute-start.13 = (f32[256,1,1]{0,2,1:T(1,128)S(1)}, f32[256,1,1]{0,2,1:T(1,128)S(1)}, u32[]{:S(2)}, u32[]{:S(2)}) collective-permute-start(f32[256,1,1]{0,2,1:T(1,128)S(1)} %get-tuple-element.47), channel_id=1, source_target_pairs={{32,1},{33,2},{34,3},{35,4},{36,5},{37,6},{38,7},{39,8},{40,9},{41... | collective-permute-start | bytes 3080 | tf_op jit(solution)/shard_map/ppermute | solution.py:32
  143.3 16.0 %collective-permute-start.14 = (f32[256,4,1]{0,2,1:T(1,128)S(1)}, f32[256,4,1]{0,2,1:T(1,128)S(1)}, u32[]{:S(2)}, u32[]{:S(2)}) collective-permute-start(f32[256,4,1]{0,2,1:T(1,128)S(1)} %get-tuple-element.50), channel_id=1, source_target_pairs={{0,32},{32,64},{64,96},{96,128},{128,160},{160,192},{192,224},{1,3... | collective-permute-start | bytes 12296 | tf_op jit(solution)/shard_map/ppermute | solution.py:21
  147.0 12.3 %collective-permute-start.15 = (f32[256,4,1]{0,2,1:T(1,128)S(1)}, f32[256,4,1]{0,2,1:T(1,128)S(1)}, u32[]{:S(2)}, u32[]{:S(2)}) collective-permute-start(f32[256,4,1]{0,2,1:T(1,128)S(1)} %get-tuple-element.51), channel_id=1, source_target_pairs={{32,0},{64,32},{96,64},{128,96},{160,128},{192,160},{224,192},{33,... | collective-permute-start | bytes 12296 | tf_op jit(solution)/shard_map/ppermute | solution.py:21
  148.3 12.3 %collective-permute-start.17 = (f32[256,1,128]{0,2,1:T(8,128)S(1)}, f32[256,1,128]{0,2,1:T(8,128)S(1)}, u32[]{:S(2)}, u32[]{:S(2)}) collective-permute-start(f32[256,1,128]{0,2,1:T(8,128)S(1)} %get-tuple-element.48), channel_id=1, source_target_pairs={{1,0},{2,1},{3,2},{4,3},{5,4},{6,5},{7,6},{8,7},{9,8},{10,9},{11,1... | collective-permute-start | bytes 393224 | tf_op jit(solution)/shard_map/ppermute | solution.py:21
  151.0 8.3 %collective-permute-start.12 = (f32[256,1,128]{0,2,1:T(8,128)S(1)}, f32[256,1,128]{0,2,1:T(8,128)S(1)}, u32[]{:S(2)}, u32[]{:S(2)}) collective-permute-start(f32[256,1,128]{0,2,1:T(8,128)S(1)} %get-tuple-element.49), channel_id=1, source_target_pairs={{0,1},{1,2},{2,3},{3,4},{4,5},{5,6},{6,7},{7,8},{8,9},{9,10},{10,1... | collective-permute-start | bytes 393224 | tf_op jit(solution)/shard_map/ppermute | solution.py:21
  155.6 5.0 %collective-permute-start.16 = (f32[256,1,1]{0,2,1:T(1,128)S(1)}, f32[256,1,1]{0,2,1:T(1,128)S(1)}, u32[]{:S(2)}, u32[]{:S(2)}) collective-permute-start(f32[256,1,1]{0,2,1:T(1,128)S(1)} %get-tuple-element.46), channel_id=1, source_target_pairs={{1,32},{2,33},{3,34},{4,35},{5,36},{6,37},{7,38},{8,39},{9,40},{10... | collective-permute-start | bytes 3080 | tf_op jit(solution)/shard_map/ppermute | solution.py:32
  159.4 3.8 %copy-start.2 = (f32[256,5,129]{0,2,1:T(8,128)S(1)}, f32[256,5,129]{0,2,1:T(8,128)}, u32[]{:S(2)}) copy-start(f32[256,5,129]{0,2,1:T(8,128)} %copy-done.1) | copy-start | bytes 1981444
  169.5 31.9 %all-to-all-start.5 = ((f32[256,1,224]{2,1,0:T(1,128)}), f32[256,1,224]{2,1,0:T(1,128)S(1)}, u32[]{:S(2)}, u32[]{:S(2)}) async-start(f32[256,1,224]{2,1,0:T(1,128)} %broadcast_in_dim_reshape.4), calls=%async_computation.5 | async-start | bytes 524288 | tf_op jit(solution)/shard_map/all_to_all | solution.py:87
  201.4 13.1 %all-to-all-start.4 = ((f32[256,4,128]{2,1,0:T(4,128)}), f32[256,4,128]{2,1,0:T(4,128)S(1)}, u32[]{:S(2)}, u32[]{:S(2)}) async-start(f32[256,4,128]{2,1,0:T(4,128)} %copy.124), calls=%async_computation.4 | async-start | bytes 1048576 | tf_op jit(solution)/shard_map/all_to_all | solution.py:161
  215.2 14.5 %all-to-all-start.6 = ((f32[64,1,224]{2,1,0:T(1,128)}), f32[64,1,224]{2,1,0:T(1,128)S(1)}, u32[]{:S(2)}, u32[]{:S(2)}) async-start(f32[64,1,224]{2,1,0:T(1,128)} %broadcast_in_dim.10), calls=%async_computation.6 | async-start | bytes 131072 | tf_op jit(solution)/shard_map/all_to_all | solution.py:95
  (6 other events, 5.5 us)
